TPU v7x, 512 devices: a whole 4x4x16 slice. The times are simulated.
512 devices in a mesh: rows: 32 (over x, y, core), cols: 16 (over z).
Axes of the slice: x: 4, y: 4, z: 16, core: 2. Of those that a mesh axis runs over, the one named last changes fastest.
Arguments:
- panel_t: float32 [256, 65536], P('cols', 'rows'), as said below
- trailing: float32 [65536, 4096], P('rows', 'cols'), may hold values from -6 to 6
- prev_lower_t: float32 [256, 65536], P('cols', 'rows'), may hold values from -6 to 6
- prev_upper: float32 [256, 4096], P(None, 'cols'), may hold values from -0.375 to 0.375
- leaf_picks: int32 [32, 256], P('rows'), may hold values from 0 to 2047, as said below
- merge_picks: int32 [31, 256], replicated, may hold values from 0 to 511, as said below
Outputs:
- lower_t: float32 [256, 65536], P('cols', 'rows')
- upper_left: float32 [256, 256], replicated
- upper_right: float32 [256, 4096], P(None, 'cols')
- updated: float32 [65536, 4096], P('rows', 'cols')
- gram: float32 [256, 256], P('cols')
Inputs may be any that keep to these rules, and one draw needn't show every extreme that they name: `leaf_picks`: each row lists 256 different row numbers within the 2048 rows of one index of rows. `merge_picks`: each row lists 256 different positions in a stack of two candidate lists. `panel_t`: the rows of the panel at the pivots form a strictly diagonally dominant block.
All inputs are finite; a program needn't handle non-finite values.
Results may differ from a plain program's by a relative error of at most 0.0003.
Values sent between devices are 32-bit elements; how exact they have to be, the bound alone decides.
No kernel may reach another device: no remote copies, remote signals or barrier semaphores. Data moves between devices by JAX's collectives and lax.ppermute only.
A program may use at most 64 MiB of HBM per device.

v0:
```python
import jax
import jax.numpy as jnp
from jax import lax
from jax.sharding import PartitionSpec as P

full_precision = lax.Precision.HIGHEST


def from_partner(shard, axis, apart):
    return lax.ppermute(shard, axis, [(i, i ^ 1 << apart) for i in range(lax.axis_size(axis))])


def trace_pivots(merge_picks, row_devices):
    list_width = merge_picks.shape[1]
    leaf_group = jnp.zeros((list_width,), jnp.int32)
    leaf_slot = jnp.arange(list_width, dtype=jnp.int32)
    levels = row_devices.bit_length() - 1
    for section in reversed(range(levels)):
        offset_rows = row_devices - (row_devices >> section)
        position = merge_picks[offset_rows + leaf_group, leaf_slot]
        right_side = (position >= list_width).astype(jnp.int32)
        leaf_group = 2 * leaf_group + right_side
        leaf_slot = position - list_width * right_side
    return (leaf_group, leaf_slot)


def product(left_side, right_side):
    return jnp.dot(left_side, right_side, precision=full_precision)


def unit_lower_inverse(lower):
    order = lower.shape[0]
    identity = jnp.eye(order, dtype=jnp.float32)
    power = identity - lower
    result = identity + power
    covered = 1
    while covered < order - 1:
        power = product(power, power)
        result = product(result, identity + power)
        covered = 2 * covered + 1
    return result


def upper_inverse(upper):
    diagonal = jnp.diagonal(upper)
    scaled = upper / diagonal[:, None]
    unit_inverse = unit_lower_inverse(scaled.T).T
    return unit_inverse / diagonal[None, :]


def small_factor(matrix):
    order = matrix.shape[0]
    row_index = lax.broadcasted_iota(jnp.int32, (order, order), 0)
    col_index = lax.broadcasted_iota(jnp.int32, (order, order), 1)
    line_index = jnp.arange(order, dtype=jnp.int32)
    reduced = matrix
    for column_index in range(order - 1):
        pivot_line = jnp.sum(jnp.where(row_index == column_index, reduced, 0.0), 0)
        pivot_column = jnp.sum(jnp.where(col_index == column_index, reduced, 0.0), 1)
        pivot_value = jnp.sum(jnp.where(line_index == column_index, pivot_line, 0.0))
        factors = jnp.where(line_index > column_index, pivot_column / pivot_value, 0.0)
        below = row_index > column_index
        reduced = jnp.where(
            below & (col_index > column_index),
            reduced - factors[:, None] * pivot_line[None, :],
            reduced,
        )
        reduced = jnp.where(below & (col_index == column_index), factors[:, None], reduced)
    return (jnp.tril(reduced, -1) + jnp.eye(order, dtype=matrix.dtype), jnp.triu(reduced))


def factor(matrix):
    order = matrix.shape[0]
    if order <= 32:
        return small_factor(matrix)
    middle_index = order // 2
    lower_head, upper_head = factor(matrix[:middle_index, :middle_index])
    upper_side = product(unit_lower_inverse(lower_head), matrix[:middle_index, middle_index:])
    lower_side = product(matrix[middle_index:, :middle_index], upper_inverse(upper_head))
    schur_block = matrix[middle_index:, middle_index:] - product(lower_side, upper_side)
    lower_tail, upper_tail = factor(schur_block)
    zero_upper = jnp.zeros((middle_index, order - middle_index), matrix.dtype)
    zero_lower = jnp.zeros((order - middle_index, middle_index), matrix.dtype)
    lower_full = jnp.concatenate(
        [
            jnp.concatenate([lower_head, zero_upper], 1),
            jnp.concatenate([lower_side, lower_tail], 1),
        ],
        0,
    )
    upper_full = jnp.concatenate(
        [
            jnp.concatenate([upper_head, upper_side], 1),
            jnp.concatenate([zero_lower, upper_tail], 1),
        ],
        0,
    )
    return (lower_full, upper_full)


def contract_first(left_side, right_side):
    return lax.dot_general(
        left_side, right_side, (((0,), (0,)), ((), ())), precision=full_precision
    )


def contract_second(left_side, right_side):
    return lax.dot_general(
        left_side, right_side, (((1,), (1,)), ((), ())), precision=full_precision
    )


def body(panel_t, trailing, prev_lower_t, prev_upper, leaf_picks, merge_picks):
    slab_rows = panel_t.shape[0]
    rows_here = panel_t.shape[1]
    row_devices = lax.axis_size("rows")
    own_row = lax.axis_index("rows")
    own_column = lax.axis_index("cols")
    leaf_group, leaf_slot = trace_pivots(merge_picks, row_devices)
    owner_mask = leaf_group == own_row
    local_rows = jnp.take(leaf_picks[0], leaf_slot)
    middle = trailing
    middle = middle - contract_first(
        lax.all_gather(prev_lower_t, "cols", axis=0, tiled=True), prev_upper
    )
    panel_full = lax.all_gather(panel_t, "cols", axis=0, tiled=True)
    middle, panel_full = (middle, panel_full)
    candidates = jnp.take(panel_t, leaf_picks[0], axis=1)
    levels = row_devices.bit_length() - 1
    for section in range(levels):
        partner = from_partner(candidates, "rows", section)
        upper_half = own_row >> section & 1
        stacked = jnp.where(
            upper_half == 0,
            jnp.concatenate([candidates, partner], 1),
            jnp.concatenate([partner, candidates], 1),
        )
        merge_index = row_devices - (row_devices >> section) + (own_row >> section + 1)
        selection = lax.dynamic_index_in_dim(merge_picks, merge_index, 0, keepdims=False)
        candidates = jnp.take(stacked, selection, axis=1)
    block_t = lax.all_gather(candidates, "cols", axis=0, tiled=True)
    lower_left, upper_left = factor(block_t.T)
    inverse = upper_inverse(upper_left)
    chosen_rows = jnp.take(middle, local_rows, axis=0)
    pivot_trailing = lax.psum(jnp.where(owner_mask[:, None], chosen_rows, 0.0), "rows")
    upper_right = product(unit_lower_inverse(lower_left), pivot_trailing)
    lower_full = jnp.dot(inverse.T, panel_full, precision=full_precision)
    lower_tile = lax.dynamic_slice_in_dim(lower_full, own_column * slab_rows, slab_rows, 0)
    updated = middle - contract_first(lower_full, upper_right)
    gram_rows = contract_second(lower_tile, lower_full)
    gram = lax.psum(gram_rows, "rows") / (rows_here * row_devices)
    return (lower_tile, upper_left, upper_right, updated, gram)


def solution(mesh):
    return jax.shard_map(
        body,
        mesh=mesh,
        in_specs=(
            P("cols", "rows"),
            P("rows", "cols"),
            P("cols", "rows"),
            P(None, "cols"),
            P("rows", None),
            P(),
        ),
        out_specs=(P("cols", "rows"), P(), P(None, "cols"), P("rows", "cols"), P("cols", None)),
        check_vma=False,
    )
```

profile of v0, /device:TPU:1, one launch (start us, length us, event | category | flops | bytes accessed | tf_op | source)
XLA Modules:
  0.0 666.7 jit_solution(18420080270595223450)
XLA Ops:
  7.2 0.7 all-gather.5.cloned.1.call-update
  8.0 1.2 copy.357
  9.2 2.5 gather_fusion.9
  11.8 2.3 gather_fusion.10
  14.1 2.3 gather_fusion.11
  16.5 2.3 gather_fusion.12
  18.9 2.3 gather_fusion.13
  21.3 0.7 gather_fusion
  22.2 8.8 %collective-permute-start = (f32[16,256]{0,1:T(8,128)S(1)}, f32[16,256]{0,1:T(8,128)S(1)}, u32[]{:S(2)}, u32[]{:S(2)}) collective-permute-start(f32[16,256]{0,1:T(8,128)S(1)} %select_bitcast_fusion.4), channel_id=1, source_target_pairs={{0,16},{16,0},{32,48},{48,32},{64,80},{80,64},{96,112},{112,96},{1... | collective-permute-start | bytes 49160 | tf_op jit(solution)/shard_map/ppermute | solution.py:10
  31.8 1.9 gather_fusion.14
  33.9 0.7 gather_fusion.16
  34.8 1.9 collective-permute-start.1
  36.7 5.1 collective-permute-done.1
  41.8 0.7 gather_fusion.17
  42.6 1.9 collective-permute-start.2
  44.6 5.7 collective-permute-done.2
  50.3 0.7 gather_fusion.18
  51.1 1.9 collective-permute-start.3
  53.1 3.8 collective-permute-done.3
  56.9 0.7 gather_fusion.19
  57.7 1.9 collective-permute-start.4
  60.2 4.8 collective-permute-done.4
  65.0 0.7 gather_fusion.20
  65.8 27.0 %all_gather.9 = f32[256,256]{1,0:T(8,128)S(1)} all-gather(f32[16,256]{1,0:T(8,128)S(1)} %select_bitcast_fusion.5), channel_id=1, replica_groups=mesh['rows'=32,'cols'=16] {'cols'}, dimensions={0}, use_global_device_ids=true | all-gather | bytes 278528 | tf_op jit(solution)/shard_map/all_gather | solution.py:141
  103.6 0.7 divide_select_fusion.240
  109.5 0.6 divide_select_fusion.236
  115.3 0.6 divide_select_fusion.232
  118.2 0.6 divide_select_fusion.230
  131.2 0.6 divide_select_fusion.221
  137.8 0.7 gather_fusion.1
  186.9 0.8 gather_fusion.2
  238.3 0.7 gather_fusion.3
  288.1 1.3 gather_fusion.4
  340.8 0.7 gather_fusion.5
  390.2 0.8 gather_fusion.6
  441.9 0.7 divide_select_fusion.31
  442.8 0.7 gather_fusion.7
  492.5 2.5 gather_fusion.8
  496.3 0.8 copy.464
  507.7 6.1 convolution_subtract_fusion.1
  513.8 1.0 gather_fusion.15
  514.8 0.8 select_select_fusion
  515.7 3.5 fusion.224
  519.2 1.7 fusion.232
  520.9 127.3 %psum.15 = f32[16,256]{1,0:T(8,128)S(1)} all-reduce(f32[16,256]{1,0:T(8,128)S(1)} %fusion.232), channel_id=1, replica_groups=mesh['rows'=32,'cols'=16] {'rows'}, use_global_device_ids=true, to_apply=%region_745.747 | all-reduce | flops 4096 | bytes 32768 | tf_op jit(solution)/shard_map/psum | solution.py:151
  648.8 3.2 all-reduce.16.cloned.1.call-done
  652.0 1.3 fusion.231
  653.3 6.6 convolution_subtract_fusion
  (1089 shorter events, 401.2 us)
Async XLA Ops:
  7.2 500.5 %copy-start = (f32[256,256]{1,0:T(8,128)S(1)}, f32[256,256]{1,0:T(8,128)}, u32[]{:S(2)}) copy-start(f32[256,256]{1,0:T(8,128)} %param.11) | copy-start | bytes 786436
  7.2 4.6 copy-start.2
  7.2 500.5 %all-gather.5.cloned.1.call-start = ((), (), s32[]{:S(2)}) async-start(), calls=%async_computation.1 | async-start | bytes 2228224 | tf_op jit(solution)/shard_map/all_gather | solution.py:124
  7.9 507.7 %all-gather.3.cloned.1.call-start = ((), (), s32[]{:S(2)}) async-start(), calls=%async_computation | async-start | bytes 2228224 | tf_op jit(solution)/shard_map/all_gather | solution.py:126
  14.1 7.1 %copy-start.1 = (s32[1,256]{1,0:T(1,128)S(1)}, s32[1,256]{1,0:T(1,128)}, u32[]{:S(2)}) copy-start(s32[1,256]{1,0:T(1,128)} %param.12) | copy-start | bytes 3076
  22.2 11.7 %collective-permute-start = (f32[16,256]{0,1:T(8,128)S(1)}, f32[16,256]{0,1:T(8,128)S(1)}, u32[]{:S(2)}, u32[]{:S(2)}) collective-permute-start(f32[16,256]{0,1:T(8,128)S(1)} %select_bitcast_fusion.4), channel_id=1, source_target_pairs={{0,16},{16,0},{32,48},{48,32},{64,80},{80,64},{96,112},{112,96},{1... | collective-permute-start | bytes 49160 | tf_op jit(solution)/shard_map/ppermute | solution.py:10
  31.0 621.0 %all-reduce.16.cloned.1.call-start = ((), (), s32[]{:S(2)}) async-start(), calls=%async_computation.2 | async-start | bytes 524288 | tf_op jit(solution)/shard_map/psum | solution.py:145
  34.8 7.0 %collective-permute-start.1 = (f32[16,256]{0,1:T(8,128)S(1)}, f32[16,256]{0,1:T(8,128)S(1)}, u32[]{:S(2)}, u32[]{:S(2)}) collective-permute-start(f32[16,256]{0,1:T(8,128)S(1)} %select_bitcast_fusion.3), channel_id=1, source_target_pairs={{0,32},{16,48},{32,0},{48,16},{64,96},{80,112},{96,64},{112,80},{1... | collective-permute-start | bytes 49160 | tf_op jit(solution)/shard_map/ppermute | solution.py:10
  42.6 7.6 %collective-permute-start.2 = (f32[16,256]{0,1:T(8,128)S(1)}, f32[16,256]{0,1:T(8,128)S(1)}, u32[]{:S(2)}, u32[]{:S(2)}) collective-permute-start(f32[16,256]{0,1:T(8,128)S(1)} %select_bitcast_fusion.2), channel_id=1, source_target_pairs={{0,64},{16,80},{32,96},{48,112},{64,0},{80,16},{96,32},{112,48},{1... | collective-permute-start | bytes 49160 | tf_op jit(solution)/shard_map/ppermute | solution.py:10
  51.1 5.7 collective-permute-start.3
  57.7 7.3 %collective-permute-start.4 = (f32[16,256]{0,1:T(8,128)S(1)}, f32[16,256]{0,1:T(8,128)S(1)}, u32[]{:S(2)}, u32[]{:S(2)}) collective-permute-start(f32[16,256]{0,1:T(8,128)S(1)} %select_bitcast_fusion), channel_id=1, source_target_pairs={{0,256},{16,272},{32,288},{48,304},{64,320},{80,336},{96,352},{112... | collective-permute-start | bytes 49160 | tf_op jit(solution)/shard_map/ppermute | solution.py:10
  513.8 1.9 copy-start.3
  519.2 140.8 %copy-start.5 = (f32[16,2048]{1,0:T(8,128)}, f32[16,2048]{1,0:T(8,128)S(1)}, u32[]{:S(2)}) copy-start(f32[16,2048]{1,0:T(8,128)S(1)} %constant_dynamic-slice_fusion) | copy-start | bytes 393220
  653.3 6.6 copy-start.4
Sparse Core Ops, SparseCore 0:
  10.1 69.7 all-gather.4
  81.9 70.5 all-gather.2
  515.7 136.2 all-reduce.15
where the time goes:
time: 674 us; the launch traced here: 667 us
  other arithmetic  362 us (54%)
  blocking collectives  154 us (23%)
  matrix products  59.6 us (9%)
  local copies, waits for them, and re-layouts  33.2 us (5%)
  waiting for transfers between devices  23.2 us (3%)
  between operations  18.1 us (3%)
  starting transfers between devices  16.6 us (2%)
    select_n x248, other arithmetic, small_factor(): jnp.where(line_index > column_index, pivot_column / pivot_value, 0.0)  161 us
    reduce_sum x248, other arithmetic, small_factor(): jnp.sum(jnp.where(line_index == column_index, pivot_line, 0.0))  151 us
    psum x1, blocking collectives, body(): gram = lax.psum(gram_rows, 'rows') / (rows_here * row_devices)  127 us
    reduce_sum x244, other arithmetic, small_factor(): jnp.sum(jnp.where(col_index == column_index, reduced, 0.0), 1)  45.1 us
    dot_general x178, matrix products, product(): return jnp.dot(left_side, right_side, precision=full_precision)  41.6 us
    all_gather x1, blocking collectives, body(): block_t = lax.all_gather(candidates, 'cols', axis=0, tiled=True)  27 us
    ppermute x5, waiting for transfers between devices, from_partner(): lax.ppermute(shard, axis, [(i, i ^ 1 << apart) for i in range(lax.axis_si...  19.3 us
    ppermute x5, starting transfers between devices, from_partner(): lax.ppermute(shard, axis, [(i, i ^ 1 << apart) for i in range(lax.axis_si...  16.5 us
  transfers between devices with their start and end apart: 8, of which 5 were waited for; matrix products, arithmetic and copies ran while one was open for 67% of the time, Pallas kernels for 0%

commit v1 on v0

--- a/solution.py
+++ b/solution.py
@@ -1,9 +1,40 @@
+import functools
 import jax
 import jax.numpy as jnp
 from jax import lax
 from jax.sharding import PartitionSpec as P
 
 full_precision = lax.Precision.HIGHEST
+
+
+def pass_thing_in(t0, d_out):
+    n_now = jax.lax.axis_size("cols")
+    outer = jax.lax.axis_index("cols")
+    now, g_now, latest = (n_now, outer, t0.shape[d_out])
+    parts_seen = []
+    for dev_i in range(now):
+        parts_seen.append((dev_i, (dev_i + 1) % now))
+    crops = []
+    for dev_i in range(now):
+        crops.append((dev_i, (dev_i - 1) % now))
+    small = jnp.zeros((*t0.shape[:d_out], now * latest, *t0.shape[d_out + 1 :]), t0.dtype)
+    small = lax.dynamic_update_slice_in_dim(small, t0, g_now * latest, axis=d_out)
+    far_arr = now // 2
+    shaped = kept_arr = t0
+    for c in range(1, far_arr + 1):
+        shaped = jax.lax.ppermute(shaped, "cols", parts_seen)
+        small = lax.dynamic_update_slice_in_dim(
+            small, shaped, (g_now - c) % now * latest, axis=d_out
+        )
+        if c < now - far_arr:
+            kept_arr = jax.lax.ppermute(kept_arr, "cols", crops)
+            small = lax.dynamic_update_slice_in_dim(
+                small, kept_arr, (g_now + c) % now * latest, axis=d_out
+            )
+    return small
+
+
+try_all_modes_over_axis = functools.partial(pass_thing_in, d_out=0)
 
 
 def from_partner(shard, axis, apart):
@@ -138,7 +169,7 @@
         merge_index = row_devices - (row_devices >> section) + (own_row >> section + 1)
         selection = lax.dynamic_index_in_dim(merge_picks, merge_index, 0, keepdims=False)
         candidates = jnp.take(stacked, selection, axis=1)
-    block_t = lax.all_gather(candidates, "cols", axis=0, tiled=True)
+    block_t = try_all_modes_over_axis(candidates)
     lower_left, upper_left = factor(block_t.T)
     inverse = upper_inverse(upper_left)
     chosen_rows = jnp.take(middle, local_rows, axis=0)

time: 674 us -> 711 us (1.055)
  starting transfers between devices: 16.6 us -> 65.9 us
  blocking collectives: 154 us -> 126 us
  waiting for transfers between devices: 23.2 us -> 33.4 us
    ppermute x0 -> x15, starting transfers between devices: none -> 49.3 us  [the longest x7 33.8 us: pass_thing_in(): kept_arr = jax.lax.ppermute(kept_arr, 'cols', crops)]
    all_gather x1 -> x0, blocking collectives: 27 us -> none  [body(): block_t = lax.all_gather(candidates, 'cols', axis=0, tiled=True)]
  transfers between devices with their start and end apart: 8 -> 23, of which waited for: 5 -> 6; matrix products, arithmetic and copies ran while one was open for 67% -> 63% of each run, Pallas kernels for 0% -> 0%
where the time goes in v1:
time: 711 us; the launch traced here: 702 us
  other arithmetic  362 us (51%)
  blocking collectives  126 us (18%)
  starting transfers between devices  65.9 us (9%)
  matrix products  60.1 us (8%)
  local copies, waits for them, and re-layouts  35 us (5%)
  waiting for transfers between devices  33.4 us (5%)
  between operations  19.3 us (3%)
    select_n x248, other arithmetic, small_factor(): jnp.where(line_index > column_index, pivot_column / pivot_value, 0.0)  161 us
    reduce_sum x248, other arithmetic, small_factor(): jnp.sum(jnp.where(line_index == column_index, pivot_line, 0.0))  151 us
    psum x1, blocking collectives, body(): gram = lax.psum(gram_rows, 'rows') / (rows_here * row_devices)  126 us
    reduce_sum x244, other arithmetic, small_factor(): jnp.sum(jnp.where(col_index == column_index, reduced, 0.0), 1)  45.1 us
    dot_general x178, matrix products, product(): return jnp.dot(left_side, right_side, precision=full_precision)  41.2 us
    ppermute x7, starting transfers between devices, pass_thing_in(): kept_arr = jax.lax.ppermute(kept_arr, 'cols', crops)  33.8 us
    ppermute x5, waiting for transfers between devices, from_partner(): lax.ppermute(shard, axis, [(i, i ^ 1 << apart) for i in range(lax.axis_si...  19.8 us
    ppermute x5, starting transfers between devices, from_partner(): lax.ppermute(shard, axis, [(i, i ^ 1 << apart) for i in range(lax.axis_si...  16.5 us
  transfers between devices with their start and end apart: 23, of which 6 were waited for; matrix products, arithmetic and copies ran while one was open for 63% of the time, Pallas kernels for 0%

profile of v1, /device:TPU:1, one launch (start us, length us, event | category | flops | bytes accessed | tf_op | source)
XLA Modules:
  0.0 701.9 jit_solution(1022512508567579775)
XLA Ops:
  8.0 1.2 copy.357
  9.2 2.5 gather_fusion.9
  11.8 2.3 gather_fusion.10
  14.1 2.3 gather_fusion.11
  16.5 2.3 gather_fusion.12
  18.9 2.3 gather_fusion.13
  22.2 8.8 %collective-permute-start = (f32[16,256]{0,1:T(8,128)S(1)}, f32[16,256]{0,1:T(8,128)S(1)}, u32[]{:S(2)}, u32[]{:S(2)}) collective-permute-start(f32[16,256]{0,1:T(8,128)S(1)} %select_bitcast_fusion.4), channel_id=1, source_target_pairs={{0,16},{16,0},{32,48},{48,32},{64,80},{80,64},{96,112},{112,96},{1... | collective-permute-start | bytes 49160 | tf_op jit(solution)/shard_map/ppermute | solution.py:41
  31.8 1.9 gather_fusion.14
  34.8 1.9 collective-permute-start.1
  36.7 5.1 collective-permute-done.1
  41.8 0.7 gather_fusion.17
  42.6 1.9 collective-permute-start.2
  44.6 5.7 collective-permute-done.2
  51.1 1.9 collective-permute-start.3
  53.1 3.8 collective-permute-done.3
  56.9 0.7 gather_fusion.19
  57.7 1.9 collective-permute-start.4
  59.7 5.3 collective-permute-done.4
  65.8 1.9 collective-permute-start.5
  67.8 6.3 collective-permute-start.6
  75.0 1.9 collective-permute-start.7
  76.9 4.6 collective-permute-start.8
  81.5 1.9 collective-permute-start.9
  83.5 4.6 collective-permute-start.10
  88.1 1.9 collective-permute-start.11
  90.0 4.6 collective-permute-start.12
  94.6 1.9 collective-permute-start.13
  96.6 4.6 collective-permute-start.14
  101.2 1.9 collective-permute-start.15
  103.1 4.6 collective-permute-start.16
  107.8 1.9 collective-permute-start.17
  109.7 4.6 collective-permute-start.18
  114.3 2.1 collective-permute-start.19
  116.5 4.1 collective-permute-done.19
  214.8 0.8 gather_fusion.2
  316.2 1.3 gather_fusion.4
  418.3 0.8 gather_fusion.6
  520.4 2.6 gather_fusion.8
  524.2 0.8 copy.464
  535.6 3.7 fusion.224
  539.4 7.0 convolution_subtract_fusion.1
  546.4 2.6 gather_fusion.15
  548.9 0.8 select_select_fusion
  549.8 1.7 fusion.232
  551.5 126.3 %psum.15 = f32[16,256]{1,0:T(8,128)S(1)} all-reduce(f32[16,256]{1,0:T(8,128)S(1)} %fusion.232), channel_id=1, replica_groups=mesh['rows'=32,'cols'=16] {'rows'}, use_global_device_ids=true, to_apply=%region_745.747 | all-reduce | flops 4096 | bytes 32768 | tf_op jit(solution)/shard_map/psum | solution.py:182
  678.4 8.7 %all-reduce.16.cloned.1.call-done = f32[256,256]{1,0:T(8,128)} async-done(((f32[256,256]{1,0:T(8,128)}), f32[256,256]{1,0:T(8,128)}) %all-reduce.16.cloned.1.call-update) | async-done | bytes 262160 | tf_op jit(solution)/shard_map/psum | solution.py:176
  687.1 1.3 fusion.231
  688.5 6.5 convolution_subtract_fusion
  (1132 shorter events, 411.4 us)
Async XLA Ops:
  7.2 532.2 %copy-start = (f32[256,256]{1,0:T(8,128)S(1)}, f32[256,256]{1,0:T(8,128)}, u32[]{:S(2)}) copy-start(f32[256,256]{1,0:T(8,128)} %param.11) | copy-start | bytes 786436
  7.2 4.6 copy-start.2
  7.2 528.4 %all-gather.3.cloned.1.call-start = ((), (), s32[]{:S(2)}) async-start(), calls=%async_computation | async-start | bytes 2228224 | tf_op jit(solution)/shard_map/all_gather | solution.py:157
  7.9 531.4 %all-gather.5.cloned.1.call-start = ((), (), s32[]{:S(2)}) async-start(), calls=%async_computation.1 | async-start | bytes 2228224 | tf_op jit(solution)/shard_map/all_gather | solution.py:155
  14.1 7.1 %copy-start.1 = (s32[1,256]{1,0:T(1,128)S(1)}, s32[1,256]{1,0:T(1,128)}, u32[]{:S(2)}) copy-start(s32[1,256]{1,0:T(1,128)} %param.12) | copy-start | bytes 3076
  22.2 11.7 %collective-permute-start = (f32[16,256]{0,1:T(8,128)S(1)}, f32[16,256]{0,1:T(8,128)S(1)}, u32[]{:S(2)}, u32[]{:S(2)}) collective-permute-start(f32[16,256]{0,1:T(8,128)S(1)} %select_bitcast_fusion.4), channel_id=1, source_target_pairs={{0,16},{16,0},{32,48},{48,32},{64,80},{80,64},{96,112},{112,96},{1... | collective-permute-start | bytes 49160 | tf_op jit(solution)/shard_map/ppermute | solution.py:41
  31.0 656.2 %all-reduce.16.cloned.1.call-start = ((), (), s32[]{:S(2)}) async-start(), calls=%async_computation.2 | async-start | bytes 524288 | tf_op jit(solution)/shard_map/psum | solution.py:176
  34.8 7.0 collective-permute-start.1
  42.6 7.6 %collective-permute-start.2 = (f32[16,256]{0,1:T(8,128)S(1)}, f32[16,256]{0,1:T(8,128)S(1)}, u32[]{:S(2)}, u32[]{:S(2)}) collective-permute-start(f32[16,256]{0,1:T(8,128)S(1)} %select_bitcast_fusion.2), channel_id=1, source_target_pairs={{0,64},{16,80},{32,96},{48,112},{64,0},{80,16},{96,32},{112,48},{1... | collective-permute-start | bytes 49160 | tf_op jit(solution)/shard_map/ppermute | solution.py:41
  51.1 5.7 collective-permute-start.3
  57.7 7.3 %collective-permute-start.4 = (f32[16,256]{0,1:T(8,128)S(1)}, f32[16,256]{0,1:T(8,128)S(1)}, u32[]{:S(2)}, u32[]{:S(2)}) collective-permute-start(f32[16,256]{0,1:T(8,128)S(1)} %select_bitcast_fusion), channel_id=1, source_target_pairs={{0,256},{16,272},{32,288},{48,304},{64,320},{80,336},{96,352},{112... | collective-permute-start | bytes 49160 | tf_op jit(solution)/shard_map/ppermute | solution.py:41
  65.8 9.1 %collective-permute-start.5 = (f32[16,256]{1,0:T(8,128)S(1)}, f32[16,256]{1,0:T(8,128)S(1)}, u32[]{:S(2)}, u32[]{:S(2)}) collective-permute-start(f32[16,256]{1,0:T(8,128)S(1)} %get-tuple-element.764), channel_id=1, source_target_pairs={{0,1},{1,2},{2,3},{3,4},{4,5},{5,6},{6,7},{7,8},{8,9},{9,10},{10,1... | collective-permute-start | bytes 49160 | tf_op jit(solution)/shard_map/ppermute | solution.py:25
  67.8 9.1 %collective-permute-start.6 = (f32[16,256]{1,0:T(8,128)S(1)}, f32[16,256]{1,0:T(8,128)S(1)}, u32[]{:S(2)}, u32[]{:S(2)}) collective-permute-start(f32[16,256]{1,0:T(8,128)S(1)} %get-tuple-element.764), channel_id=1, source_target_pairs={{0,15},{1,0},{2,1},{3,2},{4,3},{5,4},{6,5},{7,6},{8,7},{9,8},{10,9... | collective-permute-start | bytes 49160 | tf_op jit(solution)/shard_map/ppermute | solution.py:30
  75.0 6.6 collective-permute-start.7
  76.9 6.6 collective-permute-start.8
  81.5 6.6 collective-permute-start.9
  83.5 6.6 collective-permute-start.10
  88.1 6.6 collective-permute-start.11
  90.0 6.6 collective-permute-start.12
  94.6 6.6 collective-permute-start.13
  96.6 6.6 collective-permute-start.14
  101.2 6.6 collective-permute-start.15
  103.1 6.6 collective-permute-start.16
  107.8 6.6 collective-permute-start.17
  109.7 6.8 collective-permute-start.18
  114.3 6.2 collective-permute-start.19
  539.3 10.5 %copy-start.4 = (f32[16,2048]{1,0:T(8,128)}, f32[16,2048]{1,0:T(8,128)S(1)}, u32[]{:S(2)}) copy-start(f32[16,2048]{1,0:T(8,128)S(1)} %constant_dynamic-slice_fusion) | copy-start | bytes 393220
  688.5 6.5 copy-start.3
Sparse Core Ops, SparseCore 0:
  10.1 69.2 all-gather.2
  81.5 70.5 all-gather.4
  549.9 137.1 all-reduce.15
